TPU v7x, 512 devices: a whole 4x4x16 slice. The times are simulated.
512 devices in a mesh: seq: 64 (over z, y), tp: 8 (over x, core).
Axes of the slice: x: 4, y: 4, z: 16, core: 2. Of those that a mesh axis runs over, the one named last changes fastest.
Arguments:
- cache: bfloat16 [2, 64, 512, 3072], P(None, 'seq', 'tp'), may hold values from -24 to 24
- cache_len: int32 [64], replicated, may hold values from 1 to 512, 16384 in all
- group: bfloat16 [3, 64, 256, 3072], P(None, 'seq', None, 'tp'), may hold values from -24 to 24
- group_req: int32 [64], replicated, may hold values from 0 to 63, each once
- req_order: int32 [64], replicated, may hold values from 0 to 63, each once
Outputs:
- context: bfloat16 [64, 256, 3072], P('seq', None, 'tp')
Inputs may be any that keep to these rules, and one draw needn't show every extreme that they name: `group_req`: each request once. `req_order`: each request once.
All inputs are finite; a program needn't handle non-finite values.
Results may differ from a plain program's by a relative error of at most 0.0042.
Values may be sent and summed in bfloat16 or wider, within the bound.
No kernel may reach another device: no remote copies, remote signals or barrier semaphores. Data moves between devices by JAX's collectives and lax.ppermute only.
A program may use at most 64 MiB of HBM per device.

v0:
```python
import math
import jax
import jax.numpy as jnp
from jax import lax
from jax.sharding import PartitionSpec as P

HD = 96


def inverse_table(permutation):
    numbers = jnp.arange(permutation.shape[0], dtype=jnp.int32)
    matches = permutation[None, :] == numbers[:, None]
    return jnp.sum(jnp.where(matches, numbers[None, :], 0), axis=1)


def partial_part(queries, key_rows, value_rows, keep, factor):
    scores = (
        jnp.einsum("qhd,khd->hqk", queries, key_rows, preferred_element_type=jnp.float32) * factor
    )
    scores = jnp.where(keep[None], scores, -jnp.inf)
    row_top = jnp.max(scores, axis=-1)
    weights = jnp.exp(scores - row_top[..., None]).astype(jnp.bfloat16)
    weight_sum = jnp.sum(weights, axis=-1, dtype=jnp.float32)
    weighted = jnp.einsum("hqk,khd->hqd", weights, value_rows, preferred_element_type=jnp.float32)
    return (row_top, weight_sum, weighted)


def combine_parts(first_part, second_part):
    top_one, sum_one, mixed_one = first_part
    top_two, sum_two, mixed_two = second_part
    row_top = jnp.maximum(top_one, top_two)
    factor_one = jnp.exp(top_one - row_top)
    factor_two = jnp.exp(top_two - row_top)
    result = (factor_one[..., None] * mixed_one + factor_two[..., None] * mixed_two) / (
        factor_one * sum_one + factor_two * sum_two
    )[..., None]
    result = jnp.transpose(result, (1, 0, 2))
    return result.reshape(result.shape[0], -1).astype(jnp.bfloat16)


def permute_rows(rows, order):
    count = order.shape[0]
    pieces = rows.reshape(count, rows.shape[0] // count, rows.shape[1])
    spread = lax.all_to_all(pieces, "seq", split_axis=0, concat_axis=0, tiled=True)
    ordered = jnp.take(spread, order, axis=0)
    gathered = lax.all_to_all(ordered, "seq", split_axis=0, concat_axis=0, tiled=True)
    return gathered.reshape(rows.shape)


def shards(cache, cache_len, group, group_req, req_order):
    factor = 1.0 / math.sqrt(HD)
    slot_of = inverse_table(req_order)
    index_of = inverse_table(group_req)
    query_source = jnp.take(index_of, req_order)
    cache_source = jnp.take(slot_of, group_req)
    me = lax.axis_index("seq")
    slot_request = jnp.take(req_order, me)
    slot_length = jnp.take(cache_len, slot_request)
    row_count = group.shape[2]
    feature_count = group.shape[3]
    head_count = feature_count // HD
    queries = group[0, 0]
    new_keys = group[1, 0].reshape(row_count, head_count, HD)
    new_values = group[2, 0].reshape(row_count, head_count, HD)
    local = lax.all_to_all(cache[:, 0], "tp", split_axis=2, concat_axis=1, tiled=True)
    position_count = local.shape[1]
    old_keys = local[0].reshape(position_count, head_count, HD)
    old_values = local[1].reshape(position_count, head_count, HD)
    slot_queries = permute_rows(queries, query_source).reshape(row_count, head_count, HD)
    live = (jnp.arange(position_count, dtype=jnp.int32) < slot_length)[None, :]
    top_c, sum_c, mixed_c = partial_part(slot_queries, old_keys, old_values, live, factor)
    packed = jnp.concatenate(
        [
            jnp.transpose(mixed_c, (1, 0, 2)).reshape(row_count, feature_count),
            jnp.transpose(top_c),
            jnp.transpose(sum_c),
        ],
        axis=1,
    )
    back = permute_rows(packed, cache_source)
    cache_part = (
        jnp.transpose(back[:, feature_count : feature_count + head_count]),
        jnp.transpose(back[:, feature_count + head_count :]),
        jnp.transpose(back[:, :feature_count].reshape(row_count, head_count, HD), (1, 0, 2)),
    )
    causal = (
        jnp.arange(row_count, dtype=jnp.int32)[:, None]
        >= jnp.arange(row_count, dtype=jnp.int32)[None, :]
    )
    group_part = partial_part(
        queries.reshape(row_count, head_count, HD), new_keys, new_values, causal, factor
    )
    context = combine_parts(cache_part, group_part)
    return context[None]


def solution(mesh):
    in_specs = (P(None, "seq", "tp", None), P(), P(None, "seq", None, "tp"), P(), P())
    out_specs = P("seq", None, "tp")
    return jax.shard_map(shards, mesh=mesh, in_specs=in_specs, out_specs=out_specs, check_vma=False)
```

profile of v0, /device:TPU:8, one launch (start us, length us, event | category | flops | bytes accessed | tf_op | source)
XLA Modules:
  0.0 167.5 jit_solution(6261947117886503793)
XLA Ops:
  0.0 1.9 %fusion.18 = (bf16[1,1,256,384]{3,2,1,0:T(8,128)(2,1)}, bf16[1,1,256,384]{3,2,1,0:T(8,128)(2,1)S(1)}, bf16[1,1,256,384]{3,2,1,0:T(8,128)(2,1)S(1)}) fusion(bf16[3,1,256,384]{3,2,1,0:T(8,128)(2,1)} %param.9), kind=kLoop, calls=%fused_computation.52 | loop fusion | bytes 1179648 | tf_op jit(solution)/shard_map/slice | solution.py:63
  1.9 0.7 reshape_squeeze.18
  2.7 18.9 %all-to-all-start = ((bf16[64,4,384]{2,1,0:T(4,128)(2,1)}), bf16[64,4,384]{2,1,0:T(4,128)(2,1)}, u32[]{:S(2)}, u32[]{:S(2)}) async-start(bf16[64,4,384]{2,1,0:T(4,128)(2,1)} %reshape_squeeze.18), calls=%async_computation | async-start | bytes 393216 | tf_op jit(solution)/shard_map/all_to_all | solution.py:44
  21.6 1.9 %copy.45 = bf16[2,1,64,3072]{2,0,3,1:T(2,128)(2,1)S(1)} copy(bf16[2,1,64,3072]{3,2,1,0:T(8,128)(2,1)S(1)} %copy-done.1) | data formatting | bytes 1572864 | tf_op args[0]
  23.5 1.1 bitcast_bitcast_fusion
  24.7 1.9 %reshape.168 = bf16[8,2,24576]{2,1,0:T(2,128)(2,1)} reshape(bf16[3072,2,64]{2,1,0:T(2,128)(2,1)S(1)} %bitcast_bitcast_fusion) | data formatting | bytes 1572864
  26.6 14.0 %all-to-all-done = bf16[64,4,384]{2,1,0:T(4,128)(2,1)} async-done(((bf16[64,4,384]{2,1,0:T(4,128)(2,1)}), bf16[64,4,384]{2,1,0:T(4,128)(2,1)}, u32[]{:S(2)}, u32[]{:S(2)}) %all-to-all-start) | async-done | bytes 196640 | tf_op jit(solution)/shard_map/all_to_all | solution.py:44
  40.6 4.3 %all-to-all-start.2 = ((bf16[8,2,24576]{2,1,0:T(2,128)(2,1)}), bf16[8,2,24576]{2,1,0:T(2,128)(2,1)S(1)}, u32[]{:S(2)}, u32[]{:S(2)}) async-start(bf16[8,2,24576]{2,1,0:T(2,128)(2,1)} %reshape.168), calls=%async_computation.2 | async-start | bytes 1572864 | tf_op jit(solution)/shard_map/all_to_all | solution.py:65
  44.9 0.1 select_reduce_fusion
  45.0 0.8 gather_fusion.3
  45.8 1.7 %gather_fusion = bf16[64,4,384]{2,1,0:T(4,128)(2,1)S(1)} fusion(bf16[64,4,384]{2,1,0:T(4,128)(2,1)} %all-to-all-done, s32[1024]{0:T(1024)S(1)} %pad_clamp_fusion.1), kind=kCustom, calls=%fused_computation.2 | custom fusion | bytes 393472 | tf_op jit(solution)/shard_map/jit(_take)/gather | solution.py:45
  47.5 0.9 broadcast_select_fusion.1
  48.4 9.6 %all-to-all-done.2 = bf16[8,2,24576]{2,1,0:T(2,128)(2,1)S(1)} async-done(((bf16[8,2,24576]{2,1,0:T(2,128)(2,1)}), bf16[8,2,24576]{2,1,0:T(2,128)(2,1)S(1)}, u32[]{:S(2)}, u32[]{:S(2)}) %all-to-all-start.2) | async-done | bytes 786464 | tf_op jit(solution)/shard_map/all_to_all | solution.py:65
  58.0 6.4 %all-to-all-start.1 = ((bf16[64,4,384]{2,1,0:T(4,128)(2,1)}), bf16[64,4,384]{2,1,0:T(4,128)(2,1)}, u32[]{:S(2)}, u32[]{:S(2)}) async-start(bf16[64,4,384]{2,1,0:T(4,128)(2,1)} %broadcast_select_fusion.1), calls=%async_computation.1 | async-start | bytes 393216 | tf_op jit(solution)/shard_map/all_to_all | solution.py:46
  64.4 0.7 dynamic-slice.4
  65.8 0.7 dynamic-slice.5
  67.2 1.0 reshape.169
  68.2 1.2 copy.46
  69.5 0.4 reshape_squeeze.19
  69.8 0.4 reshape_squeeze.20
  70.2 13.6 %all-to-all-done.1 = bf16[64,4,384]{2,1,0:T(4,128)(2,1)} async-done(((bf16[64,4,384]{2,1,0:T(4,128)(2,1)}), bf16[64,4,384]{2,1,0:T(4,128)(2,1)}, u32[]{:S(2)}, u32[]{:S(2)}) %all-to-all-start.1) | async-done | bytes 196640 | tf_op jit(solution)/shard_map/all_to_all | solution.py:46
  83.8 1.1 reshape_reshape.3
  85.0 0.5 fusion
  85.5 0.6 convert_reduce_fusion
  86.1 0.7 convolution_bitcast_fusion.1
  86.9 0.2 copy.50
  87.1 0.4 concatenate.10
  87.5 0.1 copy.63
  87.7 0.1 copy.62
  87.8 1.0 pad_maximum_fusion
  88.8 5.5 %all-to-all-start.3 = ((f32[64,4,392]{2,1,0:T(4,128)}), f32[64,4,392]{2,1,0:T(4,128)S(1)}, u32[]{:S(2)}, u32[]{:S(2)}) async-start(f32[64,4,392]{2,1,0:T(4,128)} %pad_maximum_fusion), calls=%async_computation.3 | async-start | bytes 1048576 | tf_op jit(solution)/shard_map/all_to_all | solution.py:44
  94.3 0.1 select_reduce_fusion.1
  94.4 0.8 gather_fusion.2
  95.3 30.8 %all-to-all-done.3 = f32[64,4,392]{2,1,0:T(4,128)S(1)} async-done(((f32[64,4,392]{2,1,0:T(4,128)}), f32[64,4,392]{2,1,0:T(4,128)S(1)}, u32[]{:S(2)}, u32[]{:S(2)}) %all-to-all-start.3) | async-done | bytes 401440 | tf_op jit(solution)/shard_map/all_to_all | solution.py:44
  126.0 0.9 gather_fusion.1
  126.9 1.0 broadcast_select_fusion
  127.9 6.0 %all-to-all-start.4 = ((f32[64,4,392]{2,1,0:T(4,128)}), f32[64,4,392]{2,1,0:T(4,128)S(1)}, u32[]{:S(2)}, u32[]{:S(2)}) async-start(f32[64,4,392]{2,1,0:T(4,128)} %broadcast_select_fusion), calls=%async_computation.4 | async-start | bytes 1048576 | tf_op jit(solution)/shard_map/all_to_all | solution.py:46
  133.8 0.1 copy.54
  134.0 0.1 copy.55
  134.1 0.1 copy.57
  134.3 0.4 fusion.20
  134.7 0.2 convert_reduce_fusion.1
  134.9 30.8 %all-to-all-done.4 = f32[64,4,392]{2,1,0:T(4,128)S(1)} async-done(((f32[64,4,392]{2,1,0:T(4,128)}), f32[64,4,392]{2,1,0:T(4,128)S(1)}, u32[]{:S(2)}, u32[]{:S(2)}) %all-to-all-start.4) | async-done | bytes 401440 | tf_op jit(solution)/shard_map/all_to_all | solution.py:46
  165.7 0.2 reshape.68
  165.9 0.1 fusion.19
  166.2 0.2 copy.56
  166.4 0.3 fusion.5
  166.7 0.8 copy.60
  (25 shorter events, 0.4 us)
Async XLA Ops:
  0.0 21.6 %copy-start.1 = (bf16[2,1,64,3072]{3,2,1,0:T(8,128)(2,1)S(1)}, bf16[2,1,64,3072]{3,2,1,0:T(8,128)(2,1)}, u32[]{:S(2)}) copy-start(bf16[2,1,64,3072]{3,2,1,0:T(8,128)(2,1)} %param.7) | copy-start | bytes 2359300
  2.7 37.9 %all-to-all-start = ((bf16[64,4,384]{2,1,0:T(4,128)(2,1)}), bf16[64,4,384]{2,1,0:T(4,128)(2,1)}, u32[]{:S(2)}, u32[]{:S(2)}) async-start(bf16[64,4,384]{2,1,0:T(4,128)(2,1)} %reshape_squeeze.18), calls=%async_computation | async-start | bytes 393216 | tf_op jit(solution)/shard_map/all_to_all | solution.py:44
  23.5 3.1 %copy-start.2 = (s32[64]{0:T(128)S(1)}, s32[64]{0:T(128)}, u32[]{:S(2)}) copy-start(s32[64]{0:T(128)} %param.11) | copy-start | bytes 772
  24.7 20.2 %copy-start.3 = (s32[64]{0:T(128)S(1)}, s32[64]{0:T(128)}, u32[]{:S(2)}) copy-start(s32[64]{0:T(128)} %param.10) | copy-start | bytes 772
  26.6 39.2 %copy-start.4 = (s32[64]{0:T(128)S(1)}, s32[64]{0:T(128)}, u32[]{:S(2)}) copy-start(s32[64]{0:T(128)} %param.8) | copy-start | bytes 772
  40.6 17.4 %all-to-all-start.2 = ((bf16[8,2,24576]{2,1,0:T(2,128)(2,1)}), bf16[8,2,24576]{2,1,0:T(2,128)(2,1)S(1)}, u32[]{:S(2)}, u32[]{:S(2)}) async-start(bf16[8,2,24576]{2,1,0:T(2,128)(2,1)} %reshape.168), calls=%async_computation.2 | async-start | bytes 1572864 | tf_op jit(solution)/shard_map/all_to_all | solution.py:65
  58.0 25.8 %all-to-all-start.1 = ((bf16[64,4,384]{2,1,0:T(4,128)(2,1)}), bf16[64,4,384]{2,1,0:T(4,128)(2,1)}, u32[]{:S(2)}, u32[]{:S(2)}) async-start(bf16[64,4,384]{2,1,0:T(4,128)(2,1)} %broadcast_select_fusion.1), calls=%async_computation.1 | async-start | bytes 393216 | tf_op jit(solution)/shard_map/all_to_all | solution.py:46
  88.8 37.3 %all-to-all-start.3 = ((f32[64,4,392]{2,1,0:T(4,128)}), f32[64,4,392]{2,1,0:T(4,128)S(1)}, u32[]{:S(2)}, u32[]{:S(2)}) async-start(f32[64,4,392]{2,1,0:T(4,128)} %pad_maximum_fusion), calls=%async_computation.3 | async-start | bytes 1048576 | tf_op jit(solution)/shard_map/all_to_all | solution.py:44
  94.3 39.7 %copy-start = (bf16[1,1,256,384]{3,2,1,0:T(8,128)(2,1)S(1)}, bf16[1,1,256,384]{3,2,1,0:T(8,128)(2,1)}, u32[]{:S(2)}) copy-start(bf16[1,1,256,384]{3,2,1,0:T(8,128)(2,1)} %get-tuple-element.37) | copy-start | bytes 589828
  127.9 37.8 %all-to-all-start.4 = ((f32[64,4,392]{2,1,0:T(4,128)}), f32[64,4,392]{2,1,0:T(4,128)S(1)}, u32[]{:S(2)}, u32[]{:S(2)}) async-start(f32[64,4,392]{2,1,0:T(4,128)} %broadcast_select_fusion), calls=%async_computation.4 | async-start | bytes 1048576 | tf_op jit(solution)/shard_map/all_to_all | solution.py:46
where the time goes:
time: 168 us
  waiting for transfers between devices  98.8 us (59%)
  starting transfers between devices  41.1 us (24%)
  local copies, waits for them, and re-layouts  20.1 us (12%)
  other arithmetic  3.87 us (2%)
  matrix products  1.95 us (1%)
  between operations  1.72 us (1%)
    all_to_all x2, waiting for transfers between devices, permute_rows(): lax.all_to_all(pieces, 'seq', split_axis=0, concat_axis=0, tiled=True)  44.7 us
    all_to_all x2, waiting for transfers between devices, permute_rows(): lax.all_to_all(ordered, 'seq', split_axis=0, concat_axis=0, tiled=True)  44.5 us
    all_to_all x2, starting transfers between devices, permute_rows(): lax.all_to_all(pieces, 'seq', split_axis=0, concat_axis=0, tiled=True)  24.4 us
    all_to_all x2, starting transfers between devices, permute_rows(): lax.all_to_all(ordered, 'seq', split_axis=0, concat_axis=0, tiled=True)  12.4 us
    all_to_all x1, waiting for transfers between devices, shards(): lax.all_to_all(cache[:, 0], 'tp', split_axis=2, concat_axis=1, tiled=True)  9.63 us
    unnamed x16, local copies, waits for them, and re-layouts  6.19 us
    all_to_all x1, starting transfers between devices, shards(): lax.all_to_all(cache[:, 0], 'tp', split_axis=2, concat_axis=1, tiled=True)  4.3 us
  transfers between devices with their start and end apart: 5, of which 5 were waited for; matrix products, arithmetic and copies ran while one was open for 9% of the time, Pallas kernels for 0%

commit v1 on v0

--- a/solution.py
+++ b/solution.py
@@ -1,3 +1,4 @@
+import functools
 import math
 import jax
 import jax.numpy as jnp
@@ -5,6 +6,29 @@
 from jax.sharding import PartitionSpec as P
 
 HD = 96
+
+
+def take_pieces_all(arr, ax_name, in_dim, dim_at):
+    r_now, t1 = (jax.lax.axis_size(ax_name), jax.lax.axis_index(ax_name))
+    carry = arr.shape[in_dim] // r_now
+    part_next = list(arr.shape)
+    part_next[in_dim] = carry
+    oldest = part_next[dim_at]
+    part_next[dim_at] = oldest * r_now
+    local_part = jnp.zeros(part_next, arr.dtype)
+    for at in tuple(range(r_now)):
+        moved = lax.dynamic_slice_in_dim(arr, (t1 ^ at) * carry, carry, axis=in_dim)
+        if at:
+            moved = jax.lax.ppermute(
+                moved, axis_name=ax_name, perm=[(src_i, src_i ^ at) for src_i in range(r_now)]
+            )
+        local_part = lax.dynamic_update_slice_in_dim(
+            local_part, moved, (t1 ^ at) * oldest, axis=dim_at
+        )
+    return local_part
+
+
+balance_corner = functools.partial(take_pieces_all, ax_name="tp", in_dim=2, dim_at=1)
 
 
 def inverse_table(permutation):
@@ -62,7 +86,7 @@
     queries = group[0, 0]
     new_keys = group[1, 0].reshape(row_count, head_count, HD)
     new_values = group[2, 0].reshape(row_count, head_count, HD)
-    local = lax.all_to_all(cache[:, 0], "tp", split_axis=2, concat_axis=1, tiled=True)
+    local = balance_corner(cache[:, 0])
     position_count = local.shape[1]
     old_keys = local[0].reshape(position_count, head_count, HD)
     old_values = local[1].reshape(position_count, head_count, HD)

time: 168 us -> 177 us (1.054)
  the two profiles are of different devices: /device:TPU:8 before, /device:TPU:6 now
where the time goes in v1:
time: 177 us; the launch traced here: 176 us
  waiting for transfers between devices  80 us (45%)
  starting transfers between devices  66.7 us (38%)
  local copies, waits for them, and re-layouts  20.9 us (12%)
  other arithmetic  5.2 us (3%)
  matrix products  1.86 us (1%)
  between operations  1.86 us (1%)
    all_to_all x2, waiting for transfers between devices, permute_rows(): lax.all_to_all(pieces, 'seq', split_axis=0, concat_axis=0, tiled=True)  48.9 us
    all_to_all x2, starting transfers between devices, permute_rows(): lax.all_to_all(pieces, 'seq', split_axis=0, concat_axis=0, tiled=True)  34 us
    all_to_all x2, waiting for transfers between devices, permute_rows(): lax.all_to_all(ordered, 'seq', split_axis=0, concat_axis=0, tiled=True)  31 us
    ppermute x7, starting transfers between devices, take_pieces_all(): jax.lax.ppermute(moved, axis_name=ax_name, perm=[(src_i, src_i ^ at) for...  22.3 us
    all_to_all x2, starting transfers between devices, permute_rows(): lax.all_to_all(ordered, 'seq', split_axis=0, concat_axis=0, tiled=True)  10.5 us
    dynamic_update_slice x8, local copies, waits for them, and re-layouts, take_pieces_all(): lax.dynamic_update_slice_in_dim(local_part, moved, (t1 ^ at) * oldest, ax...  9.79 us
  transfers between devices with their start and end apart: 11, of which 3 were waited for; matrix products, arithmetic and copies ran while one was open for 10% of the time, Pallas kernels for 0%

profile of v1, /device:TPU:6, one launch (start us, length us, event | category | flops | bytes accessed | tf_op | source)
XLA Modules:
  0.0 176.4 jit_solution(7213443276418190235)
XLA Ops:
  0.0 1.2 fusion.16
  1.3 0.7 reshape_squeeze.18
  2.0 18.9 %all-to-all-start = ((bf16[64,4,384]{2,1,0:T(4,128)(2,1)}), bf16[64,4,384]{2,1,0:T(4,128)(2,1)S(1)}, u32[]{:S(2)}, u32[]{:S(2)}) async-start(bf16[64,4,384]{2,1,0:T(4,128)(2,1)} %reshape_squeeze.18), calls=%async_computation | async-start | bytes 393216 | tf_op jit(solution)/shard_map/all_to_all | solution.py:68
  20.9 0.7 compare_select_fusion
  21.5 0.8 select_reduce_fusion
  22.3 0.8 gather_fusion.3
  23.1 17.9 %all-to-all-done = bf16[64,4,384]{2,1,0:T(4,128)(2,1)S(1)} async-done(((bf16[64,4,384]{2,1,0:T(4,128)(2,1)}), bf16[64,4,384]{2,1,0:T(4,128)(2,1)S(1)}, u32[]{:S(2)}, u32[]{:S(2)}) %all-to-all-start) | async-done | bytes 196640 | tf_op jit(solution)/shard_map/all_to_all | solution.py:68
  41.1 0.8 gather_fusion
  41.8 0.9 broadcast_select_fusion.1
  42.7 4.6 %all-to-all-start.1 = ((bf16[64,4,384]{2,1,0:T(4,128)(2,1)}), bf16[64,4,384]{2,1,0:T(4,128)(2,1)S(1)}, u32[]{:S(2)}, u32[]{:S(2)}) async-start(bf16[64,4,384]{2,1,0:T(4,128)(2,1)} %broadcast_select_fusion.1), calls=%async_computation.1 | async-start | bytes 393216 | tf_op jit(solution)/shard_map/all_to_all | solution.py:70
  47.5 1.9 %collective-permute-start = (bf16[2,64,384]{2,1,0:T(8,128)(2,1)S(1)}, bf16[2,64,384]{2,1,0:T(8,128)(2,1)S(1)}, u32[]{:S(2)}, u32[]{:S(2)}) collective-permute-start(bf16[2,64,384]{2,1,0:T(8,128)(2,1)S(1)} %get-tuple-element.43), channel_id=1, source_target_pairs={{0,1},{1,0},{2,3},{3,2},{4,5},{5,4},{6,7},{7,6},{8,9},{9,8},{10,11... | collective-permute-start | bytes 294920 | tf_op jit(solution)/shard_map/ppermute | solution.py:22
  49.5 2.7 %collective-permute-start.1 = (bf16[2,64,384]{2,1,0:T(8,128)(2,1)S(1)}, bf16[2,64,384]{2,1,0:T(8,128)(2,1)S(1)}, u32[]{:S(2)}, u32[]{:S(2)}) collective-permute-start(bf16[2,64,384]{2,1,0:T(8,128)(2,1)S(1)} %get-tuple-element.42), channel_id=1, source_target_pairs={{0,2},{1,3},{2,0},{3,1},{4,6},{5,7},{6,4},{7,5},{8,10},{9,11},{10,... | collective-permute-start | bytes 294920 | tf_op jit(solution)/shard_map/ppermute | solution.py:22
  52.2 2.9 %collective-permute-start.2 = (bf16[2,64,384]{2,1,0:T(8,128)(2,1)S(1)}, bf16[2,64,384]{2,1,0:T(8,128)(2,1)S(1)}, u32[]{:S(2)}, u32[]{:S(2)}) collective-permute-start(bf16[2,64,384]{2,1,0:T(8,128)(2,1)S(1)} %get-tuple-element.41), channel_id=1, source_target_pairs={{0,3},{1,2},{2,1},{3,0},{4,7},{5,6},{6,5},{7,4},{8,11},{9,10},{10,... | collective-permute-start | bytes 294920 | tf_op jit(solution)/shard_map/ppermute | solution.py:22
  55.1 3.3 %collective-permute-start.3 = (bf16[2,64,384]{2,1,0:T(8,128)(2,1)S(1)}, bf16[2,64,384]{2,1,0:T(8,128)(2,1)S(1)}, u32[]{:S(2)}, u32[]{:S(2)}) collective-permute-start(bf16[2,64,384]{2,1,0:T(8,128)(2,1)S(1)} %get-tuple-element.40), channel_id=1, source_target_pairs={{0,4},{1,5},{2,6},{3,7},{4,0},{5,1},{6,2},{7,3},{8,12},{9,13},{10,... | collective-permute-start | bytes 294920 | tf_op jit(solution)/shard_map/ppermute | solution.py:22
  58.5 3.7 %collective-permute-start.4 = (bf16[2,64,384]{2,1,0:T(8,128)(2,1)S(1)}, bf16[2,64,384]{2,1,0:T(8,128)(2,1)S(1)}, u32[]{:S(2)}, u32[]{:S(2)}) collective-permute-start(bf16[2,64,384]{2,1,0:T(8,128)(2,1)S(1)} %get-tuple-element.39), channel_id=1, source_target_pairs={{0,5},{1,4},{2,7},{3,6},{4,1},{5,0},{6,3},{7,2},{8,13},{9,12},{10,... | collective-permute-start | bytes 294920 | tf_op jit(solution)/shard_map/ppermute | solution.py:22
  62.2 0.6 dynamic-slice.12
  63.6 0.6 dynamic-slice.13
  64.9 0.7 dynamic_update_slice.24
  65.6 2.6 %collective-permute-start.5 = (bf16[2,64,384]{2,1,0:T(8,128)(2,1)S(1)}, bf16[2,64,384]{2,1,0:T(8,128)(2,1)S(1)}, u32[]{:S(2)}, u32[]{:S(2)}) collective-permute-start(bf16[2,64,384]{2,1,0:T(8,128)(2,1)S(1)} %get-tuple-element.38), channel_id=1, source_target_pairs={{0,6},{1,7},{2,4},{3,5},{4,2},{5,3},{6,0},{7,1},{8,14},{9,15},{10,... | collective-permute-start | bytes 294920 | tf_op jit(solution)/shard_map/ppermute | solution.py:22
  68.3 5.1 %collective-permute-start.6 = (bf16[2,64,384]{2,1,0:T(8,128)(2,1)S(1)}, bf16[2,64,384]{2,1,0:T(8,128)(2,1)S(1)}, u32[]{:S(2)}, u32[]{:S(2)}) collective-permute-start(bf16[2,64,384]{2,1,0:T(8,128)(2,1)S(1)} %get-tuple-element.37), channel_id=1, source_target_pairs={{0,7},{1,6},{2,5},{3,4},{4,3},{5,2},{6,1},{7,0},{8,15},{9,14},{10,... | collective-permute-start | bytes 294920 | tf_op jit(solution)/shard_map/ppermute | solution.py:22
  73.4 0.2 copy.72
  73.6 1.4 dynamic_update_slice.25
  75.0 0.2 copy.74
  75.2 0.9 dynamic_update_slice.26
  76.3 1.6 dynamic_update_slice.27
  78.1 0.9 dynamic_update_slice.28
  79.3 1.6 dynamic_update_slice.29
  81.1 0.9 dynamic_update_slice.30
  82.2 1.6 dynamic_update_slice.31
  83.9 0.2 reshape_reshape.3
  84.1 0.5 fusion
  84.6 0.6 convert_reduce_fusion
  85.3 0.7 convolution_bitcast_fusion.1
  85.9 0.2 copy.86
  86.2 0.4 concatenate.10
  86.9 1.0 pad_maximum_fusion
  87.9 15.1 %all-to-all-start.2 = ((f32[64,4,392]{2,1,0:T(4,128)}), f32[64,4,392]{2,1,0:T(4,128)S(1)}, u32[]{:S(2)}, u32[]{:S(2)}) async-start(f32[64,4,392]{2,1,0:T(4,128)} %pad_maximum_fusion), calls=%async_computation.2 | async-start | bytes 1048576 | tf_op jit(solution)/shard_map/all_to_all | solution.py:68
  103.1 0.8 gather_fusion.2
  103.9 31.0 %all-to-all-done.2 = f32[64,4,392]{2,1,0:T(4,128)S(1)} async-done(((f32[64,4,392]{2,1,0:T(4,128)}), f32[64,4,392]{2,1,0:T(4,128)S(1)}, u32[]{:S(2)}, u32[]{:S(2)}) %all-to-all-start.2) | async-done | bytes 401440 | tf_op jit(solution)/shard_map/all_to_all | solution.py:68
  134.9 0.9 gather_fusion.1
  135.8 1.0 broadcast_select_fusion
  136.7 5.8 %all-to-all-start.3 = ((f32[64,4,392]{2,1,0:T(4,128)}), f32[64,4,392]{2,1,0:T(4,128)S(1)}, u32[]{:S(2)}, u32[]{:S(2)}) async-start(f32[64,4,392]{2,1,0:T(4,128)} %broadcast_select_fusion), calls=%async_computation.3 | async-start | bytes 1048576 | tf_op jit(solution)/shard_map/all_to_all | solution.py:70
  143.1 0.4 fusion.18
  143.6 31.0 %all-to-all-done.3 = f32[64,4,392]{2,1,0:T(4,128)S(1)} async-done(((f32[64,4,392]{2,1,0:T(4,128)}), f32[64,4,392]{2,1,0:T(4,128)S(1)}, u32[]{:S(2)}, u32[]{:S(2)}) %all-to-all-start.3) | async-done | bytes 401440 | tf_op jit(solution)/shard_map/all_to_all | solution.py:70
  174.6 0.2 reshape.72
  175.1 0.2 copy.92
  175.3 0.3 fusion.5
  175.6 0.8 copy.96
  (45 shorter events, 2.7 us)
Async XLA Ops:
  0.0 23.1 %copy-start.1 = (s32[64]{0:T(128)S(1)}, s32[64]{0:T(128)}, u32[]{:S(2)}) copy-start(s32[64]{0:T(128)} %param.11) | copy-start | bytes 772
  0.0 47.4 %copy-start = (bf16[2,1,64,3072]{3,2,1,0:T(8,128)(2,1)S(1)}, bf16[2,1,64,3072]{3,2,1,0:T(8,128)(2,1)}, u32[]{:S(2)}) copy-start(bf16[2,1,64,3072]{3,2,1,0:T(8,128)(2,1)} %param.7) | copy-start | bytes 2359300
  2.0 61.6 %copy-start.3 = (s32[64]{0:T(128)S(1)}, s32[64]{0:T(128)}, u32[]{:S(2)}) copy-start(s32[64]{0:T(128)} %param.8) | copy-start | bytes 772
  2.0 39.1 %all-to-all-start = ((bf16[64,4,384]{2,1,0:T(4,128)(2,1)}), bf16[64,4,384]{2,1,0:T(4,128)(2,1)S(1)}, u32[]{:S(2)}, u32[]{:S(2)}) async-start(bf16[64,4,384]{2,1,0:T(4,128)(2,1)} %reshape_squeeze.18), calls=%async_computation | async-start | bytes 393216 | tf_op jit(solution)/shard_map/all_to_all | solution.py:68
  42.7 41.2 %all-to-all-start.1 = ((bf16[64,4,384]{2,1,0:T(4,128)(2,1)}), bf16[64,4,384]{2,1,0:T(4,128)(2,1)S(1)}, u32[]{:S(2)}, u32[]{:S(2)}) async-start(bf16[64,4,384]{2,1,0:T(4,128)(2,1)} %broadcast_select_fusion.1), calls=%async_computation.1 | async-start | bytes 393216 | tf_op jit(solution)/shard_map/all_to_all | solution.py:70
  47.5 18.1 %collective-permute-start = (bf16[2,64,384]{2,1,0:T(8,128)(2,1)S(1)}, bf16[2,64,384]{2,1,0:T(8,128)(2,1)S(1)}, u32[]{:S(2)}, u32[]{:S(2)}) collective-permute-start(bf16[2,64,384]{2,1,0:T(8,128)(2,1)S(1)} %get-tuple-element.43), channel_id=1, source_target_pairs={{0,1},{1,0},{2,3},{3,2},{4,5},{5,4},{6,7},{7,6},{8,9},{9,8},{10,11... | collective-permute-start | bytes 294920 | tf_op jit(solution)/shard_map/ppermute | solution.py:22
  49.5 18.8 %collective-permute-start.1 = (bf16[2,64,384]{2,1,0:T(8,128)(2,1)S(1)}, bf16[2,64,384]{2,1,0:T(8,128)(2,1)S(1)}, u32[]{:S(2)}, u32[]{:S(2)}) collective-permute-start(bf16[2,64,384]{2,1,0:T(8,128)(2,1)S(1)} %get-tuple-element.42), channel_id=1, source_target_pairs={{0,2},{1,3},{2,0},{3,1},{4,6},{5,7},{6,4},{7,5},{8,10},{9,11},{10,... | collective-permute-start | bytes 294920 | tf_op jit(solution)/shard_map/ppermute | solution.py:22
  52.2 23.9 %collective-permute-start.2 = (bf16[2,64,384]{2,1,0:T(8,128)(2,1)S(1)}, bf16[2,64,384]{2,1,0:T(8,128)(2,1)S(1)}, u32[]{:S(2)}, u32[]{:S(2)}) collective-permute-start(bf16[2,64,384]{2,1,0:T(8,128)(2,1)S(1)} %get-tuple-element.41), channel_id=1, source_target_pairs={{0,3},{1,2},{2,1},{3,0},{4,7},{5,6},{6,5},{7,4},{8,11},{9,10},{10,... | collective-permute-start | bytes 294920 | tf_op jit(solution)/shard_map/ppermute | solution.py:22
  55.1 22.8 %collective-permute-start.3 = (bf16[2,64,384]{2,1,0:T(8,128)(2,1)S(1)}, bf16[2,64,384]{2,1,0:T(8,128)(2,1)S(1)}, u32[]{:S(2)}, u32[]{:S(2)}) collective-permute-start(bf16[2,64,384]{2,1,0:T(8,128)(2,1)S(1)} %get-tuple-element.40), channel_id=1, source_target_pairs={{0,4},{1,5},{2,6},{3,7},{4,0},{5,1},{6,2},{7,3},{8,12},{9,13},{10,... | collective-permute-start | bytes 294920 | tf_op jit(solution)/shard_map/ppermute | solution.py:22
  58.5 20.6 %collective-permute-start.4 = (bf16[2,64,384]{2,1,0:T(8,128)(2,1)S(1)}, bf16[2,64,384]{2,1,0:T(8,128)(2,1)S(1)}, u32[]{:S(2)}, u32[]{:S(2)}) collective-permute-start(bf16[2,64,384]{2,1,0:T(8,128)(2,1)S(1)} %get-tuple-element.39), channel_id=1, source_target_pairs={{0,5},{1,4},{2,7},{3,6},{4,1},{5,0},{6,3},{7,2},{8,13},{9,12},{10,... | collective-permute-start | bytes 294920 | tf_op jit(solution)/shard_map/ppermute | solution.py:22
  65.6 15.3 %collective-permute-start.5 = (bf16[2,64,384]{2,1,0:T(8,128)(2,1)S(1)}, bf16[2,64,384]{2,1,0:T(8,128)(2,1)S(1)}, u32[]{:S(2)}, u32[]{:S(2)}) collective-permute-start(bf16[2,64,384]{2,1,0:T(8,128)(2,1)S(1)} %get-tuple-element.38), channel_id=1, source_target_pairs={{0,6},{1,7},{2,4},{3,5},{4,2},{5,3},{6,0},{7,1},{8,14},{9,15},{10,... | collective-permute-start | bytes 294920 | tf_op jit(solution)/shard_map/ppermute | solution.py:22
  68.3 13.8 %collective-permute-start.6 = (bf16[2,64,384]{2,1,0:T(8,128)(2,1)S(1)}, bf16[2,64,384]{2,1,0:T(8,128)(2,1)S(1)}, u32[]{:S(2)}, u32[]{:S(2)}) collective-permute-start(bf16[2,64,384]{2,1,0:T(8,128)(2,1)S(1)} %get-tuple-element.37), channel_id=1, source_target_pairs={{0,7},{1,6},{2,5},{3,4},{4,3},{5,2},{6,1},{7,0},{8,15},{9,14},{10,... | collective-permute-start | bytes 294920 | tf_op jit(solution)/shard_map/ppermute | solution.py:22
  86.2 17.7 %copy-start.2 = (s32[64]{0:T(128)S(1)}, s32[64]{0:T(128)}, u32[]{:S(2)}) copy-start(s32[64]{0:T(128)} %param.10) | copy-start | bytes 772
  87.9 47.0 %all-to-all-start.2 = ((f32[64,4,392]{2,1,0:T(4,128)}), f32[64,4,392]{2,1,0:T(4,128)S(1)}, u32[]{:S(2)}, u32[]{:S(2)}) async-start(f32[64,4,392]{2,1,0:T(4,128)} %pad_maximum_fusion), calls=%async_computation.2 | async-start | bytes 1048576 | tf_op jit(solution)/shard_map/all_to_all | solution.py:68
  136.7 37.9 %all-to-all-start.3 = ((f32[64,4,392]{2,1,0:T(4,128)}), f32[64,4,392]{2,1,0:T(4,128)S(1)}, u32[]{:S(2)}, u32[]{:S(2)}) async-start(f32[64,4,392]{2,1,0:T(4,128)} %broadcast_select_fusion), calls=%async_computation.3 | async-start | bytes 1048576 | tf_op jit(solution)/shard_map/all_to_all | solution.py:70
